TPU v7x, 32 devices: a whole 2x2x4 slice. The times are simulated.
32 devices in a mesh: groups: 2 (over y), space: 8 (over z, x), tm: 2 (over core).
Axes of the slice: x: 2, y: 2, z: 4, core: 2. Of those that a mesh axis runs over, the one named last changes fastest.
Arguments:
- latents: bfloat16 [4, 16, 4, 256, 256], P('groups', 'space', 'tm'), parts along dimension 0, may hold values from -6 to 6
- cotangent: bfloat16 [4, 16, 4, 256, 256], P('groups', 'space', 'tm'), parts along dimension 0, may hold values from -6 to 6
- valid_frames: int32 [4], P('groups'), parts along dimension 0, may hold values from 1 to 16, as said below
- spatial_weight: bfloat16 [9, 256, 256], replicated, may hold values from -0.125 to 0.125
- temporal_weight: bfloat16 [3, 256, 256], replicated, may hold values from -0.21875 to 0.21875
- cond_weight: bfloat16 [256, 256], replicated, may hold values from -0.375 to 0.375
Outputs:
- output: bfloat16 [4, 16, 4, 256, 256], P('groups', 'space', 'tm'), parts along dimension 0
- grad_latents: bfloat16 [4, 16, 4, 256, 256], P('groups', 'space', 'tm'), parts along dimension 0
- grad_spatial: bfloat16 [18, 256, 256], P('groups'), parts along dimension 0
- grad_temporal: bfloat16 [6, 256, 256], P('groups'), parts along dimension 0
- grad_cond: bfloat16 [512, 256], P('groups'), parts along dimension 0
There are 2 independent parts, one for each index of `groups`. A program takes and returns all parts, laid end to end along the dimension named above; an argument that names none is the same for every part. Nothing has to cross between parts.
Inputs may be any that keep to these rules, and one draw needn't show every extreme that they name: `valid_frames`: the first clip has all 16 frames valid; the others have 1 to 16.
All inputs are finite; a program needn't handle non-finite values.
Results may differ from a plain program's by a relative error of at most 0.0055.
Values may be sent and summed in bfloat16 or wider, within the bound.
No kernel may reach another device: no remote copies, remote signals or barrier semaphores. Data moves between devices by JAX's collectives and lax.ppermute only.
A program may use at most 128 MiB of HBM per device.

v0:
```python
import jax
import jax.numpy as jnp
from jax import lax
from jax.sharding import PartitionSpec as P


def from_root(block, axis, source):
    block = jnp.where(lax.axis_index(axis) == source, block, jnp.zeros_like(block))
    return lax.psum(block, axis)


def shifted(value, axis, by):
    count = lax.axis_size(axis)
    pairs = [(i, i + by) for i in range(count) if 0 <= i + by < count]
    return lax.ppermute(value, axis, pairs)


def spatial_sum(padded, weights, flip):
    rows = padded.shape[2] - 2
    cols = padded.shape[3] - 2
    total = jnp.zeros(padded.shape[:2] + (rows, cols, weights.shape[2]), jnp.float32)
    for row_off in range(3):
        for col_off in range(3):
            if flip:
                piece = padded[
                    :, :, 2 - row_off : 2 - row_off + rows, 2 - col_off : 2 - col_off + cols
                ]
                kernel = weights[3 * row_off + col_off].T
            else:
                piece = padded[:, :, row_off : row_off + rows, col_off : col_off + cols]
                kernel = weights[3 * row_off + col_off]
            total = total + jnp.dot(piece, kernel, preferred_element_type=jnp.float32)
    return total


def lag_forward(padded_act, weights, count):
    total = 0.0
    for lag in range(3):
        total = total + jnp.dot(
            padded_act[:, 2 - lag : 2 - lag + count],
            weights[lag],
            preferred_element_type=jnp.float32,
        )
    return total


def lag_backward(padded_cot, weights, count):
    total = 0.0
    for lag in range(3):
        total = total + jnp.dot(
            padded_cot[:, lag : lag + count], weights[lag].T, preferred_element_type=jnp.float32
        )
    return total


def lag_grads(padded_act, cot, count):
    dims = (((0, 1, 2, 3), (0, 1, 2, 3)), ((), ()))
    terms = []
    for lag in range(3):
        terms.append(
            lax.dot_general(
                padded_act[:, 2 - lag : 2 - lag + count],
                cot,
                dims,
                preferred_element_type=jnp.float32,
            )
        )
    return jnp.stack(terms)


def own_window(whole, rows):
    padded_rows = jnp.pad(whole, ((0, 0), (0, 0), (1, 1), (0, 0), (0, 0)))
    start = lax.axis_index("tm") * rows
    return lax.dynamic_slice_in_dim(padded_rows, start, rows + 2, 2)


def on_device(latents, cotangent, valid_frames, spatial_weight, temporal_weight, cond_weight):
    clips, frames, rows, cols, chans = latents.shape
    slab = lax.axis_index("space")
    frame_ids = slab * frames + jnp.arange(frames, dtype=jnp.int32)
    mask = (frame_ids[None, :] < valid_frames[:, None]).astype(jnp.bfloat16)[:, :, None, None, None]
    mask_f = mask.astype(jnp.float32)
    masked = latents * mask
    first = from_root(masked[:, 0], "space", 0)
    rows_pad = own_window(lax.all_gather(masked, "tm", axis=2, tiled=True), rows)
    padded = jnp.pad(rows_pad, ((0, 0), (0, 0), (0, 0), (1, 1), (0, 0)))
    pre = spatial_sum(padded, spatial_weight, False)
    act = jax.nn.silu(pre).astype(jnp.bfloat16)
    cot = cotangent * mask
    earlier = shifted(act, "space", 1)
    act_pad = jnp.concatenate([earlier, act], axis=1)
    mixed = lag_forward(act_pad, temporal_weight, frames)
    later = shifted(cot, "space", -1)
    cot_pad = jnp.concatenate([cot, later], axis=1)
    dact = lag_backward(cot_pad, temporal_weight, frames)
    temporal_terms = lag_grads(act_pad, cot, frames)
    cond = jnp.dot(first, cond_weight, preferred_element_type=jnp.float32)
    output = ((masked.astype(jnp.float32) + mixed + cond[:, None]) * mask_f).astype(jnp.bfloat16)
    sig = jax.nn.sigmoid(pre)
    dpre = (dact * sig * (1.0 + pre * (1.0 - sig))).astype(jnp.bfloat16)
    cot_sum = lax.psum(jnp.sum(cot, axis=1, dtype=jnp.float32), "space")
    cond_back = jnp.dot(cot_sum, cond_weight.astype(jnp.float32).T, precision=lax.Precision.HIGHEST)
    dpre_rows = own_window(lax.all_gather(dpre, "tm", axis=2, tiled=True), rows)
    dpre_pad = jnp.pad(dpre_rows, ((0, 0), (0, 0), (0, 0), (1, 1), (0, 0)))
    dmasked = spatial_sum(dpre_pad, spatial_weight, True)
    is_first = (frame_ids == 0).astype(jnp.float32)[None, :, None, None, None]
    grad_latents = (
        (cot.astype(jnp.float32) + dmasked + is_first * cond_back[:, None]) * mask_f
    ).astype(jnp.bfloat16)
    dims = (((0, 1, 2, 3), (0, 1, 2, 3)), ((), ()))
    spatial_terms = []
    for row_off in range(3):
        for col_off in range(3):
            piece = padded[:, :, row_off : row_off + rows, col_off : col_off + cols]
            spatial_terms.append(
                lax.dot_general(piece, dpre, dims, preferred_element_type=jnp.float32)
            )
    spatial_terms = jnp.stack(spatial_terms)
    is_owner = (slab == 0).astype(jnp.float32)
    cond_terms = is_owner * lax.dot_general(
        first.astype(jnp.float32),
        cot_sum,
        (((0, 1, 2), (0, 1, 2)), ((), ())),
        precision=lax.Precision.HIGHEST,
    )
    summed = lax.psum((spatial_terms, temporal_terms, cond_terms), ("space", "tm"))
    scale = (clips * frames * rows * cols * lax.axis_size("space") * lax.axis_size("tm")) ** (-0.5)
    grad_spatial = (summed[0] * scale).astype(jnp.bfloat16)
    grad_temporal = (summed[1] * scale).astype(jnp.bfloat16)
    grad_cond = (summed[2] * scale).astype(jnp.bfloat16)
    return (output, grad_latents, grad_spatial, grad_temporal, grad_cond)


def solution(mesh):
    return jax.shard_map(
        on_device,
        mesh=mesh,
        in_specs=(
            P("groups", "space", "tm", None, None),
            P("groups", "space", "tm", None, None),
            P("groups"),
            P(),
            P(),
            P(),
        ),
        out_specs=(
            P("groups", "space", "tm", None, None),
            P("groups", "space", "tm", None, None),
            P("groups", None, None),
            P("groups", None, None),
            P("groups", None),
        ),
        check_vma=False,
    )
```

profile of v0, /device:TPU:0, one launch (start us, length us, event | category | flops | bytes accessed | tf_op | source)
XLA Modules:
  0.0 338.7 jit_solution(10557166967447815481)
XLA Ops:
  8.1 0.7 fusion.124
  8.8 1.4 broadcast_multiply_fusion.1
  10.2 0.9 fusion.44
  11.2 2.7 convert_reduce_fusion
  14.0 0.5 all-gather.3.cloned.1.call-update
  14.5 1.3 collective-permute-start.1
  15.9 1.8 fusion.75
  17.7 75.7 %all-reduce.9.cloned.1.call-done = bf16[2,2,256,256]{3,2,1,0:T(8,128)(2,1)} async-done(((bf16[2,2,256,256]{3,2,1,0:T(8,128)(2,1)}), bf16[2,2,256,256]{3,2,1,0:T(8,128)(2,1)}) %all-reduce.9.cloned.1.call-update) | async-done | bytes 524304 | tf_op jit(solution)/shard_map/psum | solution.py:9
  93.3 2.3 fusion.47
  95.7 79.6 %all-reduce.11.cloned.1.call-done = f32[2,2,256,256]{3,2,1,0:T(8,128)} async-done(((f32[2,2,256,256]{3,2,1,0:T(8,128)}), f32[2,2,256,256]{3,2,1,0:T(8,128)}) %all-reduce.11.cloned.1.call-update) | async-done | bytes 1048592 | tf_op jit(solution)/shard_map/psum | solution.py:101
  175.3 3.0 fusion.13
  178.2 1.6 fusion.45
  179.9 1.8 fusion.3
  181.7 1.8 pad_dynamic-slice_fusion.1
  183.5 0.4 fusion.38
  183.9 0.5 fusion.39
  184.4 0.5 fusion.40
  184.8 0.5 fusion.41
  185.3 0.5 fusion.42
  185.8 0.5 fusion.43
  186.2 0.4 fusion.59
  186.6 0.4 fusion.67
  187.1 2.1 multiply_convert_fusion.3
  189.4 0.5 copy-done.24
  189.9 2.0 multiply_convert_fusion.1
  191.9 1.2 fusion.19
  193.2 3.5 %collective-permute-start = (bf16[2,2,2,256,256]{4,3,2,1,0:T(8,128)(2,1)}, bf16[2,2,2,256,256]{4,3,2,1,0:T(8,128)(2,1)S(1)}, u32[]{:S(2)}, u32[]{:S(2)}) collective-permute-start(bf16[2,2,2,256,256]{4,3,2,1,0:T(8,128)(2,1)} %get-tuple-element.12), channel_id=1, source_target_pairs={{0,2},{2,4},{4,6},{6,8},{8,10},{10,12},{12,14},{1,3},{3,5},{5,7},{... | collective-permute-start | bytes 3145736 | tf_op jit(solution)/shard_map/ppermute | solution.py:15
  196.7 2.4 fusion.12
  199.1 1.2 fusion.18
  200.3 1.2 fusion.17
  201.5 1.2 fusion.11
  202.7 1.2 fusion.16
  203.8 1.2 fusion.15
  205.1 0.4 copy-done.7
  205.5 0.5 convolution_bitcast_fusion.5
  205.9 1.2 fusion.10
  207.1 1.2 fusion.14
  208.3 2.7 fusion.77
  211.0 7.8 %collective-permute-done = bf16[2,2,2,256,256]{4,3,2,1,0:T(8,128)(2,1)S(1)} collective-permute-done((bf16[2,2,2,256,256]{4,3,2,1,0:T(8,128)(2,1)}, bf16[2,2,2,256,256]{4,3,2,1,0:T(8,128)(2,1)S(1)}, u32[]{:S(2)}, u32[]{:S(2)}) %collective-permute-start) | collective-permute-done | bytes 1048608 | tf_op jit(solution)/shard_map/ppermute | solution.py:15
  218.9 0.5 convolution_bitcast_fusion.4
  219.3 0.5 fusion.9
  219.8 1.0 pad_maximum_fusion.5
  220.8 1.2 copy-done.8
  222.0 0.3 copy-done.10
  222.4 0.4 fusion.7
  222.9 0.8 copy-done.12
  223.7 0.7 copy-done.13
  224.6 1.7 multiply_convert_fusion.2
  226.3 1.8 pad_dynamic-slice_fusion
  228.2 0.5 fusion.20
  228.6 0.5 fusion.22
  229.1 0.5 fusion.24
  229.6 0.5 fusion.26
  230.1 0.5 fusion.28
  230.6 0.5 fusion.30
  231.1 0.5 fusion.57
  231.6 0.5 fusion.65
  232.0 0.8 copy-done.6
  232.8 0.3 copy-done.16
  233.1 2.2 fusion.2
  235.3 91.7 %all-reduce.13.cloned.1.call-done = (f32[9,256,256]{2,1,0:T(8,128)}, f32[3,256,256]{2,1,0:T(8,128)}, f32[256,256]{1,0:T(8,128)}) async-done(((f32[9,256,256]{2,1,0:T(8,128)}, f32[3,256,256]{2,1,0:T(8,128)}, f32[256,256]{1,0:T(8,128)}), (f32[9,256,256]{2,1,0:T(8,128)}, f32[3,256,256]{2,1,0:T(8,128)}, f32[256,256]{1,0:T(8,128)})) %all-reduce.13.cloned.1.call-update) | async-done | bytes 3407888 | tf_op jit(solution)/shard_map/psum | solution.py:126
  327.0 3.0 multiply_convert_fusion
  330.0 0.8 multiply_convert_fusion.4
  330.9 0.7 multiply_convert_fusion.5
  (60 shorter events, 0.9 us)
Async XLA Ops:
  8.0 85.3 %copy-start = (bf16[256,256]{1,0:T(8,128)(2,1)S(1)}, bf16[256,256]{1,0:T(8,128)(2,1)}, u32[]{:S(2)}) copy-start(bf16[256,256]{1,0:T(8,128)(2,1)} %param.11) | copy-start | bytes 393220
  8.0 85.3 %all-reduce.9.cloned.1.call-start = ((), (), s32[]{:S(2)}) async-start(), calls=%async_computation.1 | async-start | bytes 1048576 | tf_op jit(solution)/shard_map/psum | solution.py:9
  10.2 3.7 %copy-start.11 = (bf16[2,2,2,256,256]{4,3,2,1,0:T(8,128)(2,1)}, bf16[2,2,2,256,256]{4,3,2,1,0:T(8,128)(2,1)S(1)}, u32[]{:S(2)}) copy-start(bf16[2,2,2,256,256]{4,3,2,1,0:T(8,128)(2,1)S(1)} %broadcast_multiply_fusion.1) | copy-start | bytes 3145732
  11.1 4.8 %copy-start.21 = (bf16[3,256,256]{2,1,0:T(8,128)(2,1)S(1)}, bf16[3,256,256]{2,1,0:T(8,128)(2,1)}, u32[]{:S(2)}) copy-start(bf16[3,256,256]{2,1,0:T(8,128)(2,1)} %param.10) | copy-start | bytes 1179652
  11.1 164.2 %all-reduce.11.cloned.1.call-start = ((), (), s32[]{:S(2)}) async-start(), calls=%async_computation.3 | async-start | bytes 2097152 | tf_op jit(solution)/shard_map/psum | solution.py:101
  13.9 166.0 %copy-start.4 = (bf16[2,2,2,256,256]{4,3,2,1,0:T(8,128)(2,1)}, bf16[2,2,2,256,256]{4,3,2,1,0:T(8,128)(2,1)S(1)}, u32[]{:S(2)}) copy-start(bf16[2,2,2,256,256]{4,3,2,1,0:T(8,128)(2,1)S(1)} %get-tuple-element.9) | copy-start | bytes 3145732
  13.9 167.8 %all-gather.3.cloned.1.call-start = ((), (), s32[]{:S(2)}) async-start(), calls=%async_computation | async-start | bytes 3145728 | tf_op jit(solution)/shard_map/all_gather | solution.py:85
  14.5 211.8 %all-gather.5.cloned.1.call-start = ((), (), s32[]{:S(2)}) async-start(), calls=%async_computation.2 | async-start | bytes 3145728 | tf_op jit(solution)/shard_map/all_gather | solution.py:103
  14.5 165.3 %collective-permute-start.1 = (bf16[2,2,2,256,256]{4,3,2,1,0:T(8,128)(2,1)S(1)}, bf16[2,2,2,256,256]{4,3,2,1,0:T(8,128)(2,1)S(1)}, u32[]{:S(2)}, u32[]{:S(2)}) collective-permute-start(bf16[2,2,2,256,256]{4,3,2,1,0:T(8,128)(2,1)S(1)} %get-tuple-element.9), channel_id=1, source_target_pairs={{2,0},{4,2},{6,4},{8,6},{10,8},{12,10},{14,12},{3,1},{5,3},{7,5},{... | collective-permute-start | bytes 3145736 | tf_op jit(solution)/shard_map/ppermute | solution.py:15
  175.3 3.0 copy-start.18
  179.8 1.8 copy-start.23
  181.7 1.8 copy-start.14
  187.1 2.2 copy-start.19
  187.1 2.3 copy-start.20
  187.1 2.8 copy-start.24
  191.9 1.2 copy-start.2
  193.1 6.0 %copy-start.3 = (bf16[2,2,2,256,256]{4,3,2,1,0:T(8,128)(2,1)S(1)}, bf16[2,2,2,256,256]{4,3,2,1,0:T(8,128)(2,1)}, u32[]{:S(2)}) copy-start(bf16[2,2,2,256,256]{4,3,2,1,0:T(8,128)(2,1)} %copy-done.2) | copy-start | bytes 3145732
  193.2 133.8 %all-reduce.13.cloned.1.call-start = ((), (), s32[]{:S(2)}) async-start(), calls=%async_computation.4 | async-start | bytes 6815744 | tf_op jit(solution)/shard_map/psum | solution.py:126
  193.2 25.7 %collective-permute-start = (bf16[2,2,2,256,256]{4,3,2,1,0:T(8,128)(2,1)}, bf16[2,2,2,256,256]{4,3,2,1,0:T(8,128)(2,1)S(1)}, u32[]{:S(2)}, u32[]{:S(2)}) collective-permute-start(bf16[2,2,2,256,256]{4,3,2,1,0:T(8,128)(2,1)} %get-tuple-element.12), channel_id=1, source_target_pairs={{0,2},{2,4},{4,6},{6,8},{8,10},{10,12},{12,14},{1,3},{3,5},{5,7},{... | collective-permute-start | bytes 3145736 | tf_op jit(solution)/shard_map/ppermute | solution.py:15
  203.8 1.2 copy-start.5
  203.8 1.6 copy-start.7
  218.9 1.0 copy-start.9
  220.8 1.2 copy-start.8
  220.8 1.5 copy-start.10
  220.8 1.6 copy-start.22
  222.4 1.2 copy-start.12
  222.4 1.9 copy-start.13
  222.4 2.2 copy-start.17
  226.3 1.9 copy-start.15
  231.6 1.2 copy-start.6
  231.6 1.6 copy-start.16
  327.0 3.0 copy-start.25
  327.0 4.5 %copy-start.1 = (bf16[256,256]{1,0:T(8,128)(2,1)S(1)}, bf16[256,256]{1,0:T(8,128)(2,1)}, u32[]{:S(2)}) copy-start(bf16[256,256]{1,0:T(8,128)(2,1)} %param.11) | copy-start | bytes 393220
  327.0 3.9 %copy-start.26 = (f32[256,256]{1,0:T(8,128)S(1)}, f32[256,256]{1,0:T(8,128)}, u32[]{:S(2)}) copy-start(f32[256,256]{1,0:T(8,128)} %get-tuple-element.7) | copy-start | bytes 786436
Sparse Core Ops, SparseCore 0:
  12.8 80.4 all-reduce.8
  97.8 77.4 all-reduce.10
  220.9 105.9 all-reduce.12
Sparse Core Ops, SparseCore 1:
  16.5 13.1 all-gather.2
  193.2 10.0 all-gather.4
where the time goes:
time: 339 us
  waiting for transfers between devices  255 us (75%)
  matrix products  42.3 us (12%)
  between operations  15.5 us (5%)
  other arithmetic  11.2 us (3%)
  local copies, waits for them, and re-layouts  9.27 us (3%)
  starting transfers between devices  5.03 us (1%)
    psum x1, waiting for transfers between devices, on_device(): lax.psum((spatial_terms, temporal_terms, cond_terms), ('space', 'tm'))  91.7 us
    psum x1, waiting for transfers between devices, on_device(): cot_sum = lax.psum(jnp.sum(cot, axis=1, dtype=jnp.float32), 'space')  79.6 us
    psum x1, waiting for transfers between devices, from_root(): return lax.psum(block, axis)  75.7 us
    dot_general x9, matrix products, on_device(): lax.dot_general(piece, dpre, dims, preferred_element_type=jnp.float32)  11.9 us
    dot_general x18, matrix products, spatial_sum(): total = total + jnp.dot(piece, kernel, preferred_element_type=jnp.float32)  11.7 us
    ppermute x2, waiting for transfers between devices, shifted(): return lax.ppermute(value, axis, pairs)  7.84 us
  transfers between devices with their start and end apart: 7, of which 4 were waited for; matrix products, arithmetic and copies ran while one was open for 12% of the time, Pallas kernels for 0%

commit v1 on v0

--- a/solution.py
+++ b/solution.py
@@ -123,7 +123,8 @@
         (((0, 1, 2), (0, 1, 2)), ((), ())),
         precision=lax.Precision.HIGHEST,
     )
-    summed = lax.psum((spatial_terms, temporal_terms, cond_terms), ("space", "tm"))
+    inner = lax.psum((spatial_terms, temporal_terms, cond_terms), "tm")
+    summed = lax.psum(inner, "space")
     scale = (clips * frames * rows * cols * lax.axis_size("space") * lax.axis_size("tm")) ** (-0.5)
     grad_spatial = (summed[0] * scale).astype(jnp.bfloat16)
     grad_temporal = (summed[1] * scale).astype(jnp.bfloat16)

time: 339 us -> 393 us (1.16)
  waiting for transfers between devices: 255 us -> 316 us
  matrix products: 42.3 us -> 37.4 us
    psum x1 -> x2, waiting for transfers between devices: 91.7 us -> 132 us  [the longest x1 117 us: on_device(): summed = lax.psum(inner, 'space')]
    all_gather x1, waiting for transfers between devices: 0.01 us -> 13.2 us  [on_device(): dpre_rows = own_window(lax.all_gather(dpre, 'tm', axis=2, tiled=True), rows)]
    dot_general x9, matrix products: 11.9 us -> 4.35 us  [on_device(): lax.dot_general(piece, dpre, dims, preferred_element_type=jnp.float32)]
    ppermute x2, waiting for transfers between devices: 7.84 us -> 12.5 us  [shifted(): return lax.ppermute(value, axis, pairs)]
  transfers between devices with their start and end apart: 7 -> 8, of which waited for: 4 -> 6; matrix products, arithmetic and copies ran while one was open for 12% -> 8% of each run, Pallas kernels for 0% -> 0%
where the time goes in v1:
time: 393 us
  waiting for transfers between devices  316 us (80%)
  matrix products  37.4 us (10%)
  between operations  15.8 us (4%)
  other arithmetic  11.2 us (3%)
  local copies, waits for them, and re-layouts  6.24 us (2%)
  starting transfers between devices  5.9 us (2%)
    psum x1, waiting for transfers between devices, on_device(): summed = lax.psum(inner, 'space')  117 us
    psum x1, waiting for transfers between devices, on_device(): cot_sum = lax.psum(jnp.sum(cot, axis=1, dtype=jnp.float32), 'space')  81.9 us
    psum x1, waiting for transfers between devices, from_root(): return lax.psum(block, axis)  75.1 us
    psum x1, waiting for transfers between devices, on_device(): inner = lax.psum((spatial_terms, temporal_terms, cond_terms), 'tm')  15.4 us
    all_gather x1, waiting for transfers between devices, on_device(): dpre_rows = own_window(lax.all_gather(dpre, 'tm', axis=2, tiled=True), rows)  13.2 us
    ppermute x2, waiting for transfers between devices, shifted(): return lax.ppermute(value, axis, pairs)  12.5 us
    dot_general x18, matrix products, spatial_sum(): total = total + jnp.dot(piece, kernel, preferred_element_type=jnp.float32)  11.9 us
  transfers between devices with their start and end apart: 8, of which 6 were waited for; matrix products, arithmetic and copies ran while one was open for 8% of the time, Pallas kernels for 0%

profile of v1, /device:TPU:0, one launch (start us, length us, event | category | flops | bytes accessed | tf_op | source)
XLA Modules:
  0.0 392.5 jit_solution(5136906398002696829)
XLA Ops:
  8.1 0.7 fusion.124
  8.8 1.4 broadcast_multiply_fusion.1
  10.2 0.9 fusion.44
  11.2 2.7 convert_reduce_fusion
  14.0 0.5 all-gather.3.cloned.1.call-update
  14.6 1.3 collective-permute-start.1
  15.9 1.8 fusion.75
  17.7 75.1 %all-reduce.11.cloned.1.call-done = bf16[2,2,256,256]{3,2,1,0:T(8,128)(2,1)} async-done(((bf16[2,2,256,256]{3,2,1,0:T(8,128)(2,1)}), bf16[2,2,256,256]{3,2,1,0:T(8,128)(2,1)}) %all-reduce.11.cloned.1.call-update) | async-done | bytes 524304 | tf_op jit(solution)/shard_map/psum | solution.py:9
  92.9 81.9 %all-reduce.13.cloned.1.call-done = f32[2,2,256,256]{3,2,1,0:T(8,128)} async-done(((f32[2,2,256,256]{3,2,1,0:T(8,128)}), f32[2,2,256,256]{3,2,1,0:T(8,128)}) %all-reduce.13.cloned.1.call-update) | async-done | bytes 1048592 | tf_op jit(solution)/shard_map/psum | solution.py:101
  174.8 2.9 fusion.13
  177.7 1.1 copy-done.16
  178.8 1.8 fusion.3
  180.6 1.8 pad_dynamic-slice_fusion.1
  182.4 0.5 fusion.38
  182.8 0.4 fusion.39
  183.3 0.5 fusion.40
  183.7 0.5 fusion.41
  184.2 0.5 fusion.42
  184.6 0.5 fusion.43
  185.1 0.4 fusion.59
  185.5 0.4 fusion.67
  186.0 2.2 multiply_convert_fusion.3
  188.1 4.1 %collective-permute-start = (bf16[2,2,2,256,256]{4,3,2,1,0:T(8,128)(2,1)}, bf16[2,2,2,256,256]{4,3,2,1,0:T(8,128)(2,1)}, u32[]{:S(2)}, u32[]{:S(2)}) collective-permute-start(bf16[2,2,2,256,256]{4,3,2,1,0:T(8,128)(2,1)} %get-tuple-element.15), channel_id=1, source_target_pairs={{0,2},{2,4},{4,6},{6,8},{8,10},{10,12},{12,14},{1,3},{3,5},{5,7},{... | collective-permute-start | bytes 3145736 | tf_op jit(solution)/shard_map/ppermute | solution.py:15
  192.3 2.0 multiply_convert_fusion.1
  194.3 0.5 fusion.19
  194.8 0.5 fusion.12
  195.3 0.5 fusion.18
  195.8 0.5 fusion.17
  196.2 0.5 fusion.11
  196.7 0.5 fusion.16
  197.2 0.7 copy-done.3
  198.0 1.7 convolution_bitcast_fusion.5
  199.7 0.5 fusion.15
  200.2 0.5 fusion.10
  200.6 0.5 fusion.14
  201.2 12.5 %collective-permute-done = bf16[2,2,2,256,256]{4,3,2,1,0:T(8,128)(2,1)} collective-permute-done((bf16[2,2,2,256,256]{4,3,2,1,0:T(8,128)(2,1)}, bf16[2,2,2,256,256]{4,3,2,1,0:T(8,128)(2,1)}, u32[]{:S(2)}, u32[]{:S(2)}) %collective-permute-start) | collective-permute-done | bytes 1048608 | tf_op jit(solution)/shard_map/ppermute | solution.py:15
  213.7 1.7 fusion.9
  215.4 1.7 convolution_bitcast_fusion.4
  217.1 0.9 pad_maximum_fusion.5
  218.1 0.5 all-gather.5.cloned.1.call-update
  218.6 0.3 all-reduce.15.cloned.1.call-start
  218.9 0.1 copy-done.13
  219.0 0.3 fusion.47
  219.4 0.6 fusion.45
  220.0 1.7 fusion.77
  221.7 1.7 fusion.7
  223.4 3.2 multiply_convert_fusion.2
  226.7 15.4 %all-reduce.17.cloned.1.call-done = (f32[9,256,256]{2,1,0:T(8,128)}, f32[3,256,256]{2,1,0:T(8,128)}, f32[256,256]{1,0:T(8,128)}) async-done(((f32[9,256,256]{2,1,0:T(8,128)}, f32[3,256,256]{2,1,0:T(8,128)}, f32[256,256]{1,0:T(8,128)}), (f32[9,256,256]{2,1,0:T(8,128)}, f32[3,256,256]{2,1,0:T(8,128)}, f32[256,256]{1,0:T(8,128)})) %all-reduce.17.cloned.1.call-update) | async-done | bytes 3407888 | tf_op jit(solution)/shard_map/psum | solution.py:126
  242.1 13.2 %all-gather.5.cloned.1.call-done = bf16[2,2,4,256,256]{4,3,2,1,0:T(8,128)(2,1)} async-done(((bf16[2,2,2,256,256]{4,3,2,1,0:T(8,128)(2,1)}), bf16[2,2,4,256,256]{4,3,2,1,0:T(8,128)(2,1)}) %all-gather.5.cloned.1.call-update) | async-done | bytes 2097168 | tf_op jit(solution)/shard_map/all_gather | solution.py:103
  255.3 1.7 pad_dynamic-slice_fusion
  256.9 0.5 fusion.20
  257.4 0.5 fusion.22
  257.9 0.5 fusion.24
  258.4 0.5 fusion.26
  258.9 0.5 fusion.28
  259.4 0.5 fusion.30
  259.9 0.5 fusion.57
  260.4 0.5 fusion.65
  260.8 0.8 copy-done.4
  261.6 2.4 fusion.2
  263.9 116.7 %all-reduce.15.cloned.1.call-done = (f32[9,256,256]{2,1,0:T(8,128)}, f32[3,256,256]{2,1,0:T(8,128)}, f32[256,256]{1,0:T(8,128)}) async-done(((f32[9,256,256]{2,1,0:T(8,128)}, f32[3,256,256]{2,1,0:T(8,128)}, f32[256,256]{1,0:T(8,128)}), (f32[9,256,256]{2,1,0:T(8,128)}, f32[3,256,256]{2,1,0:T(8,128)}, f32[256,256]{1,0:T(8,128)})) %all-reduce.15.cloned.1.call-update) | async-done | bytes 3407888 | tf_op jit(solution)/shard_map/psum | solution.py:127
  380.6 3.0 multiply_convert_fusion
  383.7 0.8 multiply_convert_fusion.4
  384.5 0.7 multiply_convert_fusion.5
  (49 shorter events, 0.4 us)
Async XLA Ops:
  8.0 210.9 %copy-start = (bf16[256,256]{1,0:T(8,128)(2,1)S(1)}, bf16[256,256]{1,0:T(8,128)(2,1)}, u32[]{:S(2)}) copy-start(bf16[256,256]{1,0:T(8,128)(2,1)} %param.11) | copy-start | bytes 393220
  8.0 84.9 %all-reduce.11.cloned.1.call-start = ((), (), s32[]{:S(2)}) async-start(), calls=%async_computation.1 | async-start | bytes 1048576 | tf_op jit(solution)/shard_map/psum | solution.py:9
  10.2 3.7 copy-start.5
  11.1 4.8 %copy-start.14 = (bf16[3,256,256]{2,1,0:T(8,128)(2,1)S(1)}, bf16[3,256,256]{2,1,0:T(8,128)(2,1)}, u32[]{:S(2)}) copy-start(bf16[3,256,256]{2,1,0:T(8,128)(2,1)} %param.10) | copy-start | bytes 1179652
  11.1 163.7 %all-reduce.13.cloned.1.call-start = ((), (), s32[]{:S(2)}) async-start(), calls=%async_computation.3 | async-start | bytes 2097152 | tf_op jit(solution)/shard_map/psum | solution.py:101
  13.9 163.8 %copy-start.2 = (bf16[2,2,2,256,256]{4,3,2,1,0:T(8,128)(2,1)}, bf16[2,2,2,256,256]{4,3,2,1,0:T(8,128)(2,1)S(1)}, u32[]{:S(2)}) copy-start(bf16[2,2,2,256,256]{4,3,2,1,0:T(8,128)(2,1)S(1)} %get-tuple-element.12) | copy-start | bytes 3145732
  13.9 166.7 %all-gather.3.cloned.1.call-start = ((), (), s32[]{:S(2)}) async-start(), calls=%async_computation | async-start | bytes 3145728 | tf_op jit(solution)/shard_map/all_gather | solution.py:85
  14.5 227.5 %all-reduce.17.cloned.1.call-start = ((), (), s32[]{:S(2)}) async-start(), calls=%async_computation.5 | async-start | bytes 6815744 | tf_op jit(solution)/shard_map/psum | solution.py:126
  14.6 163.1 %collective-permute-start.1 = (bf16[2,2,2,256,256]{4,3,2,1,0:T(8,128)(2,1)S(1)}, bf16[2,2,2,256,256]{4,3,2,1,0:T(8,128)(2,1)S(1)}, u32[]{:S(2)}, u32[]{:S(2)}) collective-permute-start(bf16[2,2,2,256,256]{4,3,2,1,0:T(8,128)(2,1)S(1)} %get-tuple-element.12), channel_id=1, source_target_pairs={{2,0},{4,2},{6,4},{8,6},{10,8},{12,10},{14,12},{3,1},{5,3},{7,5},{... | collective-permute-start | bytes 3145736 | tf_op jit(solution)/shard_map/ppermute | solution.py:15
  177.7 1.1 copy-start.16
  180.6 1.8 copy-start.7
  186.0 6.3 %copy-start.11 = (f32[2,2,2,256,256]{4,3,2,1,0:T(8,128)S(1)}, f32[2,2,2,256,256]{4,3,2,1,0:T(8,128)}, u32[]{:S(2)}) copy-start(f32[2,2,2,256,256]{4,3,2,1,0:T(8,128)} %fusion.75) | copy-start | bytes 6291460
  186.0 6.3 %copy-start.12 = (f32[2,2,2,256,256]{4,3,2,1,0:T(8,128)S(1)}, f32[2,2,2,256,256]{4,3,2,1,0:T(8,128)}, u32[]{:S(2)}) copy-start(f32[2,2,2,256,256]{4,3,2,1,0:T(8,128)} %fusion.3) | copy-start | bytes 6291460
  186.0 6.3 %copy-start.17 = (bf16[2,2,2,256,256]{4,3,2,1,0:T(8,128)(2,1)S(1)}, bf16[2,2,2,256,256]{4,3,2,1,0:T(8,128)(2,1)}, u32[]{:S(2)}) copy-start(bf16[2,2,2,256,256]{4,3,2,1,0:T(8,128)(2,1)} %copy-done.16) | copy-start | bytes 3145732
  188.1 25.5 %collective-permute-start = (bf16[2,2,2,256,256]{4,3,2,1,0:T(8,128)(2,1)}, bf16[2,2,2,256,256]{4,3,2,1,0:T(8,128)(2,1)}, u32[]{:S(2)}, u32[]{:S(2)}) collective-permute-start(bf16[2,2,2,256,256]{4,3,2,1,0:T(8,128)(2,1)} %get-tuple-element.15), channel_id=1, source_target_pairs={{0,2},{2,4},{4,6},{6,8},{8,10},{10,12},{12,14},{1,3},{3,5},{5,7},{... | collective-permute-start | bytes 3145736 | tf_op jit(solution)/shard_map/ppermute | solution.py:15
  194.3 6.4 %copy-start.1 = (bf16[2,2,2,256,256]{4,3,2,1,0:T(8,128)(2,1)}, bf16[2,2,2,256,256]{4,3,2,1,0:T(8,128)(2,1)S(1)}, u32[]{:S(2)}) copy-start(bf16[2,2,2,256,256]{4,3,2,1,0:T(8,128)(2,1)S(1)} %multiply_convert_fusion.1) | copy-start | bytes 3145732
  196.7 1.2 copy-start.3
  201.1 15.9 %copy-start.10 = (f32[9,256,256]{2,1,0:T(8,128)}, f32[9,256,256]{2,1,0:T(8,128)S(1)}, u32[]{:S(2)}) copy-start(f32[9,256,256]{2,1,0:T(8,128)S(1)} %fusion.14) | copy-start | bytes 7077892
  218.0 1.0 copy-start.13
  218.0 1.4 copy-start.9
  218.0 37.2 %all-gather.5.cloned.1.call-start = ((), (), s32[]{:S(2)}) async-start(), calls=%async_computation.2 | async-start | bytes 3145728 | tf_op jit(solution)/shard_map/all_gather | solution.py:103
  218.6 1.4 copy-start.15
  218.6 162.0 %all-reduce.15.cloned.1.call-start = ((), (), s32[]{:S(2)}) async-start(), calls=%async_computation.4 | async-start | bytes 6815744 | tf_op jit(solution)/shard_map/psum | solution.py:127
  221.7 1.7 copy-start.6
  242.1 14.9 %copy-start.8 = (bf16[9,256,256]{2,1,0:T(8,128)(2,1)S(1)}, bf16[9,256,256]{2,1,0:T(8,128)(2,1)}, u32[]{:S(2)}) copy-start(bf16[9,256,256]{2,1,0:T(8,128)(2,1)} %param.9) | copy-start | bytes 3538948
  260.3 1.2 copy-start.4
  380.6 3.0 copy-start.18
  380.6 3.9 copy-start.19
Sparse Core Ops, SparseCore 0:
  12.3 80.5 all-reduce.10
  97.4 77.4 all-reduce.12
  242.2 138.3 all-reduce.14
Sparse Core Ops, SparseCore 1:
  16.5 13.1 all-gather.2
  218.1 23.9 all-reduce.16
  243.5 11.7 all-gather.4
